TPU v7x, 256 devices: a whole 4x4x8 slice. The times are simulated.
256 devices in a mesh: batch: 8 (over z), replica: 32 (over y, x, core).
Axes of the slice: x: 4, y: 4, z: 8, core: 2. Of those that a mesh axis runs over, the one named last changes fastest.
Arguments:
- patches: bfloat16 [32, 64, 64, 1024], P('replica', 'batch'), may hold values from -6 to 6
- visible_order: int32 [32, 64, 64], P('replica', 'batch'), may hold values from 0 to 63, each once within a row
- visible_counts: int32 [32, 64], P('replica'), may hold values from 1 to 32, as said below
- dest_rows: int32 [32, 64], P('replica'), may hold values from 0 to 1023, as said below
- qkv_weight: bfloat16 [1024, 3072], P('replica')
- out_weight: bfloat16 [1024, 1024], P('replica'), may hold values from -0.1875 to 0.1875
- norm_gain: bfloat16 [1024], P('replica'), may hold values from 0.5 to 1.5
- upstream: bfloat16 [32, 1024, 1024], P('replica', 'batch'), may hold values from -6 to 6
Outputs:
- layer_out: bfloat16 [32, 1024, 1024], P('replica', 'batch')
- d_packed: bfloat16 [32, 1024, 1024], P('replica', 'batch')
- grad_qkv: float32 [1024, 3072], P('replica')
- grad_out: float32 [1024, 1024], P('replica')
- grad_gain: float32 [1024], P('replica')
Inputs may be any that keep to these rules, and one draw needn't show every extreme that they name: `visible_counts`: in every replica index, each batch index b packs exactly 128 rows: the volumes with dest_rows // 128 == b, one from every device of the batch axis, in order of that device's batch index, without gaps; one of them has 32 visible patches. `dest_rows`: the 8 volumes of one device go to 8 different batch indices; a volume's rows never cross a multiple of 128.
All inputs are finite; a program needn't handle non-finite values.
Results may differ from a plain program's by a relative error of at most 0.033.
Values may be sent and summed in bfloat16 or wider, within the bound.
No kernel may reach another device: no remote copies, remote signals or barrier semaphores. Data moves between devices by JAX's collectives and lax.ppermute only.
A program may use at most 128 MiB of HBM per device.

v0:
```python
import jax
import jax.numpy as jnp
from jax import lax
from jax.sharding import PartitionSpec as P

HEADS = 16
MAXVIS = 32
MEANVIS = 16
EPS = 1e-06
NEG = -1e30


def layer_core(tokens, upward, allowed, wqkv, wout, gain):
    groups, length, width = tokens.shape
    rows = groups * length
    head_dim = width // HEADS
    scale = head_dim ** (-0.5)
    x32 = tokens.astype(jnp.float32).reshape(rows, width)
    row_average = jnp.mean(x32, axis=1, keepdims=True)
    centered_rows = x32 - row_average
    inverse_deviation = lax.rsqrt(
        jnp.mean(centered_rows * centered_rows, axis=1, keepdims=True) + EPS
    )
    standardized_rows = centered_rows * inverse_deviation
    gain_float32 = gain.astype(jnp.float32)
    layernorm_output = (standardized_rows * gain_float32).astype(jnp.bfloat16)
    qkv = jnp.dot(layernorm_output, wqkv, preferred_element_type=jnp.float32).astype(jnp.bfloat16)
    query = qkv[:, :width].reshape(groups, length, HEADS, head_dim)
    keys = qkv[:, width : 2 * width].reshape(groups, length, HEADS, head_dim)
    values = qkv[:, 2 * width :].reshape(groups, length, HEADS, head_dim)
    scores = jnp.einsum("gqhd,gkhd->ghqk", query, keys, preferred_element_type=jnp.float32) * scale
    scores = jnp.where(allowed[:, None], scores, NEG)
    top = jnp.max(scores, axis=-1, keepdims=True)
    expd = jnp.exp(scores - top)
    probs = expd / jnp.sum(expd, axis=-1, keepdims=True)
    weights = probs.astype(jnp.bfloat16)
    context = (
        jnp.einsum("ghqk,gkhd->gqhd", weights, values, preferred_element_type=jnp.float32)
        .astype(jnp.bfloat16)
        .reshape(rows, width)
    )
    result = (x32 + jnp.dot(context, wout, preferred_element_type=jnp.float32)).astype(jnp.bfloat16)
    up_rows = upward.reshape(rows, width)
    d_context = lax.dot_general(
        up_rows, wout, (((1,), (1,)), ((), ())), preferred_element_type=jnp.float32
    ).astype(jnp.bfloat16)
    d_context = d_context.reshape(groups, length, HEADS, head_dim)
    d_values = jnp.einsum(
        "ghqk,gqhd->gkhd", weights, d_context, preferred_element_type=jnp.float32
    ).astype(jnp.bfloat16)
    d_weights = jnp.einsum("gqhd,gkhd->ghqk", d_context, values, preferred_element_type=jnp.float32)
    d_scores = (
        probs * (d_weights - jnp.sum(d_weights * probs, axis=-1, keepdims=True)) * scale
    ).astype(jnp.bfloat16)
    d_query = jnp.einsum(
        "ghqk,gkhd->gqhd", d_scores, keys, preferred_element_type=jnp.float32
    ).astype(jnp.bfloat16)
    d_keys = jnp.einsum(
        "ghqk,gqhd->gkhd", d_scores, query, preferred_element_type=jnp.float32
    ).astype(jnp.bfloat16)
    d_qkv = jnp.concatenate(
        [d_query.reshape(rows, width), d_keys.reshape(rows, width), d_values.reshape(rows, width)],
        axis=1,
    )
    layernorm_gradient = lax.dot_general(
        d_qkv, wqkv, (((1,), (1,)), ((), ())), preferred_element_type=jnp.float32
    )
    gain_products = jnp.sum(layernorm_gradient * standardized_rows, axis=0)
    normalized_gradient = layernorm_gradient * gain_float32
    input_gradient = inverse_deviation * (
        normalized_gradient
        - jnp.mean(normalized_gradient, axis=1, keepdims=True)
        - standardized_rows
        * jnp.mean(normalized_gradient * standardized_rows, axis=1, keepdims=True)
    )
    d_tokens = (up_rows.astype(jnp.float32) + input_gradient).astype(jnp.bfloat16)
    return (
        result.reshape(tokens.shape),
        d_tokens.reshape(tokens.shape),
        layernorm_output,
        context,
        d_qkv,
        up_rows,
        gain_products,
    )


def left_product(left, right):
    return lax.dot_general(
        left, right, (((0,), (0,)), ((), ())), preferred_element_type=jnp.float32
    )


def on_device(
    patches, visible_order, visible_counts, dest_rows, qkv_weight, out_weight, norm_gain, upstream
):
    qkv_cols = qkv_weight.shape[1]
    out_cols = out_weight.shape[1]
    gain_block = jnp.broadcast_to(norm_gain[:, None], (norm_gain.shape[0], 128))
    gathered = lax.all_gather(
        jnp.concatenate([qkv_weight, out_weight, gain_block], axis=1), "replica", axis=0, tiled=True
    )
    wqkv = gathered[:, :qkv_cols]
    wout = gathered[:, qkv_cols : qkv_cols + out_cols]
    gain = gathered[:, qkv_cols + out_cols]
    batches = lax.axis_size("batch")
    me_index = lax.axis_index("batch")
    cap = MEANVIS * batches
    width = wout.shape[1]
    slot = jnp.arange(MAXVIS, dtype=jnp.int32)
    sources = jnp.arange(batches, dtype=jnp.int32)
    counts_all = visible_counts[0].reshape(batches, batches)
    rows_all = dest_rows[0].reshape(batches, batches)
    mine = rows_all // cap == me_index
    src_count = jnp.sum(jnp.where(mine, counts_all, 0), axis=1)
    src_start = jnp.sum(jnp.where(mine, rows_all % cap, 0), axis=1)
    position = jnp.arange(cap, dtype=jnp.int32)
    hit = (position[:, None] >= src_start[None, :]) & (
        position[:, None] < (src_start + src_count)[None, :]
    )
    segment = jnp.sum(jnp.where(hit, sources[None, :], 0), axis=1)
    inside = jnp.sum(jnp.where(hit, position[:, None] - src_start[None, :], 0), axis=1)
    flat_rows = segment * MAXVIS + inside
    my_targets = jnp.take(rows_all, me_index, axis=0) // cap
    to_target = jnp.sum(
        jnp.where(my_targets[None, :] == sources[:, None], sources[None, :], 0), axis=1
    )
    my_counts = jnp.take(counts_all, me_index, axis=0)
    local_rows = jnp.take_along_axis(patches[0], visible_order[0, :, :MAXVIS, None], axis=1)
    live = slot[None, :] < src_count[:, None]
    pick = jnp.clip(src_start[:, None] + slot[None, :], 0, cap - 1)
    fetched = jnp.take(upstream[0], pick.reshape(-1), axis=0).reshape(batches, MAXVIS, width)
    backward_rows = jnp.where(live[..., None], fetched, jnp.zeros_like(fetched))
    returned = lax.all_to_all(backward_rows, "batch", split_axis=0, concat_axis=0, tiled=True)
    upward = jnp.take(returned, my_targets, axis=0)
    valid = slot[None, :] < my_counts[:, None]
    allowed = jnp.broadcast_to(valid[:, None, :], (batches, MAXVIS, MAXVIS))
    result, d_tokens, layernorm_output, context, d_qkv, up_rows, gain_products = layer_core(
        local_rows, upward, allowed, wqkv, wout, gain
    )
    came = lax.all_to_all(
        jnp.take(jnp.concatenate([result, d_tokens], axis=-1), to_target, axis=0),
        "batch",
        split_axis=0,
        concat_axis=0,
        tiled=True,
    )
    came_out = came[..., :width]
    came_grad = came[..., width:]
    layer_out = jnp.take(came_out.reshape(batches * MAXVIS, width), flat_rows, axis=0)
    d_packed = jnp.take(came_grad.reshape(batches * MAXVIS, width), flat_rows, axis=0)
    partial = jnp.concatenate(
        [
            left_product(layernorm_output, d_qkv).astype(jnp.bfloat16),
            left_product(context, up_rows).astype(jnp.bfloat16),
            jnp.broadcast_to(gain_products.astype(jnp.bfloat16)[:, None], (width, 128)),
        ],
        axis=1,
    )
    summed = lax.psum_scatter(partial, "replica", scatter_dimension=0, tiled=True)
    summed = lax.psum(summed, "batch").astype(jnp.float32)
    grad_q = summed[:, :qkv_cols]
    grad_o = summed[:, qkv_cols : qkv_cols + out_cols]
    grad_g = summed[:, qkv_cols + out_cols]
    return (layer_out[None], d_packed[None], grad_q, grad_o, grad_g)


def solution(mesh):
    placed = (
        P("replica", "batch", None, None),
        P("replica", "batch", None),
        P("replica", None),
        P("replica", None),
        P("replica", None),
        P("replica", None),
        P("replica"),
        P("replica", "batch", None),
    )
    return jax.shard_map(
        on_device,
        mesh=mesh,
        in_specs=placed,
        out_specs=(
            P("replica", "batch", None),
            P("replica", "batch", None),
            P("replica", None),
            P("replica", None),
            P("replica"),
        ),
        check_vma=False,
    )
```

profile of v0, /device:TPU:2, one launch (start us, length us, event | category | flops | bytes accessed | tf_op | source)
XLA Modules:
  0.0 334.6 jit_solution(9900112664250814567)
XLA Ops:
  15.7 8.5 %all-to-all-start = ((bf16[8,32,1024]{2,1,0:T(8,128)(2,1)}), bf16[8,32,1024]{2,1,0:T(8,128)(2,1)S(1)}, u32[]{:S(2)}, u32[]{:S(2)}) async-start(bf16[8,32,1024]{2,1,0:T(8,128)(2,1)} %select_select_fusion), calls=%async_computation | async-start | bytes 1048576 | tf_op jit(solution)/shard_map/all_to_all | solution.py:134
  24.3 2.8 gather_fusion.3
  28.2 13.4 %all-to-all-done = bf16[8,32,1024]{2,1,0:T(8,128)(2,1)S(1)} async-done(((bf16[8,32,1024]{2,1,0:T(8,128)(2,1)}), bf16[8,32,1024]{2,1,0:T(8,128)(2,1)S(1)}, u32[]{:S(2)}, u32[]{:S(2)}) %all-to-all-start) | async-done | bytes 524320 | tf_op jit(solution)/shard_map/all_to_all | solution.py:134
  43.3 29.1 %all-gather.2.cloned.1.call-done = bf16[1024,4224]{1,0:T(8,128)(2,1)} async-done(((bf16[32,4224]{1,0:T(8,128)(2,1)}), bf16[1024,4224]{1,0:T(8,128)(2,1)}) %all-gather.2.cloned.1.call-update) | async-done | bytes 8650768 | tf_op jit(solution)/shard_map/all_gather | solution.py:100
  72.4 3.2 fusion.43
  78.4 4.7 %fusion.6 = bf16[256,3072]{1,0:T(8,128)(2,1)S(1)} fusion(bf16[1024,4224]{1,0:T(8,128)(2,1)} %all-gather.2.cloned.1.call-done, f32[1024]{0:T(1024)S(1)} %convert_reduce_fusion.1, f32[256]{0:T(256)S(1)} %rsqrt.12, f32[256]{0:T(256)S(1)} %div.51, bf16[256,1024]{1,0:T(8,128)(2,1)S(1)} %gather_fusion.3, pred[256]{0:T(512)(128)(4,1)S(1)} %compare_and_fusion.4), kind=kOutput, calls=%fused_computation.14 | convolution fusion | flops 1612972032 | bytes 8395008 | tf_op jit(solution)/shard_map/dot_general | solution.py:27
  84.4 2.5 reshape.302
  86.9 2.5 reshape.304
  89.4 2.5 reshape.303
  91.9 3.2 fusion.66
  95.1 4.1 %fusion.111 = (f32[8,16,32]{2,1,0:T(8,128)S(1)}, f32[8,16,32,32]{2,3,1,0:T(8,128)}) fusion(pred[8,32]{1,0:T(8,128)(4,1)S(1)} %iota_compare_fusion.3, bf16[8,32,16,64]{3,2,1,0:T(8,128)(2,1)} %reshape.304, bf16[8,32,16,64]{3,2,1,0:T(8,128)(2,1)} %reshape.303), kind=kOutput, calls=%fused_computation.155 | convolution fusion | flops 17301536 | bytes 1589504 | tf_op jit(solution)/shard_map/sub | solution.py:34
  99.2 5.8 %fusion.34 = bf16[8,32,16,64]{3,1,2,0:T(8,128)(2,1)} fusion(f32[8,16,32,32]{2,3,1,0:T(8,128)} %fusion.66, bf16[8,32,16,64]{3,2,1,0:T(8,128)(2,1)} %reshape.304, f32[8,16,32,32]{2,3,1,0:T(8,128)} %get-tuple-element.37, f32[8,16,32]{2,1,0:T(8,128)S(1)} %get-tuple-element.36), kind=kOutput, calls=%fused_computation.35 | convolution fusion | flops 17960992 | bytes 2113536 | tf_op jit(solution)/shard_map/ghqk,gkhd->gqhd/dot_general | solution.py:55
  104.9 5.6 %fusion.31 = bf16[8,32,16,64]{3,1,2,0:T(8,128)(2,1)} fusion(f32[8,16,32,32]{2,3,1,0:T(8,128)} %fusion.66, bf16[8,32,16,64]{3,2,1,0:T(8,128)(2,1)} %reshape.303, f32[8,16,32,32]{2,3,1,0:T(8,128)} %get-tuple-element.37, f32[8,16,32]{2,1,0:T(8,128)S(1)} %get-tuple-element.36), kind=kOutput, calls=%fused_computation.34 | convolution fusion | flops 17960992 | bytes 2113536 | tf_op jit(solution)/shard_map/ghqk,gqhd->gkhd/dot_general | solution.py:58
  110.6 3.2 fusion.30
  117.3 1.9 constant_dynamic-update-slice_fusion.2
  128.7 1.9 constant_dynamic-update-slice_fusion.1
  130.7 1.9 constant_dynamic-update-slice_fusion
  132.6 3.5 %convolution_convert_fusion = bf16[1024,3072]{1,0:T(8,128)(2,1)S(1)} fusion(bf16[256,3072]{1,0:T(8,128)(2,1)} %constant_dynamic-update-slice_fusion, f32[1024]{0:T(1024)S(1)} %convert_reduce_fusion.1, f32[256]{0:T(256)S(1)} %rsqrt.12, f32[256]{0:T(256)S(1)} %div.51, bf16[256,1024]{1,0:T(8,128)(2,1)S(1)} %gather_fusion.3, pred[256]{0:T(512)(128)(4,1)S(1)} %compare_and_fusion.4), kind=kOutput, calls=%fused_computation.9 | convolution fusion | flops 1615331328 | bytes 8395008 | tf_op jit(solution)/shard_map/dot_general | solution.py:89
  137.5 5.8 %fusion.57 = (bf16[1024]{0:T(1024)(128)(2,1)S(1)}, f32[256]{0:T(256)S(1)}, f32[256]{0:T(256)S(1)}, f32[256,1024]{1,0:T(8,128)}) fusion(f32[256]{0:T(256)S(1)} %rsqrt.12, f32[256]{0:T(256)S(1)} %div.51, bf16[256,1024]{1,0:T(8,128)(2,1)S(1)} %gather_fusion.3, pred[256]{0:T(512)(128)(4,1)S(1)} %compare_and_fusion.4, f32[1024]{0:T(1024)S(1)} %convert_reduce_fusion.1, ...), kind=kOutput, calls=%fused_computation.53 | convolution fusion | flops 1613232640 | bytes 9447680 | tf_op jit(solution)/shard_map/dot_general | solution.py:65
  143.5 3.7 %pad_maximum_fusion = bf16[1024,4224]{1,0:T(8,128)(2,1)} fusion(bf16[1024,128]{1,0:T(8,128)(2,1)S(1)} %broadcast_in_dim.181, bf16[1024,1024]{1,0:T(8,128)(2,1)S(1)} %convolution_convert_fusion.1, bf16[1024,3072]{1,0:T(8,128)(2,1)S(1)} %convolution_convert_fusion), kind=kLoop, calls=%fused_computation.8 | loop fusion | flops 25952256 | bytes 17301504 | tf_op jit(solution)/shard_map/concatenate | solution.py:152
  149.2 2.3 fusion.40
  153.4 7.0 %all-to-all-start.1 = ((bf16[8,32,2048]{2,1,0:T(8,128)(2,1)}), bf16[8,32,2048]{2,1,0:T(8,128)(2,1)S(1)}, u32[]{:S(2)}, u32[]{:S(2)}) async-start(bf16[8,32,2048]{2,1,0:T(8,128)(2,1)} %broadcast_select_fusion), calls=%async_computation.1 | async-start | bytes 2097152 | tf_op jit(solution)/shard_map/all_to_all | solution.py:141
  160.5 87.6 %reduce-scatter.2.cloned.1.call-done = bf16[32,4224]{1,0:T(8,128)(2,1)} async-done(((bf16[1024,4224]{1,0:T(8,128)(2,1)}), bf16[32,4224]{1,0:T(8,128)(2,1)}) %reduce-scatter.2.cloned.1.call-update) | async-done | bytes 270352 | tf_op jit(solution)/shard_map/reduce_scatter | solution.py:160
  250.8 72.4 %all-reduce.2.cloned.1.call-done = bf16[32,4224]{1,0:T(8,128)(2,1)} async-done(((bf16[32,4224]{1,0:T(8,128)(2,1)}), bf16[32,4224]{1,0:T(8,128)(2,1)}) %all-reduce.2.cloned.1.call-update) | async-done | bytes 270352 | tf_op jit(solution)/shard_map/psum | solution.py:161
  (96 shorter events, 41.4 us)
Async XLA Ops:
  7.2 17.1 %copy-start = (bf16[1,8,64,1024]{3,2,1,0:T(8,128)(2,1)S(1)}, bf16[1,8,64,1024]{3,2,1,0:T(8,128)(2,1)}, u32[]{:S(2)}) copy-start(bf16[1,8,64,1024]{3,2,1,0:T(8,128)(2,1)} %param.12) | copy-start | bytes 3145732
  7.2 6.3 %copy-start.1 = (bf16[1,128,1024]{2,1,0:T(8,128)(2,1)S(1)}, bf16[1,128,1024]{2,1,0:T(8,128)(2,1)}, u32[]{:S(2)}) copy-start(bf16[1,128,1024]{2,1,0:T(8,128)(2,1)} %param.19) | copy-start | bytes 786436
  7.2 65.2 %all-gather.2.cloned.1.call-start = ((), (), s32[]{:S(2)}) async-start(), calls=%async_computation.3 | async-start | bytes 8921088 | tf_op jit(solution)/shard_map/all_gather | solution.py:100
  14.6 9.6 %copy-start.7 = (s32[1,8,64]{2,1,0:T(8,128)S(1)}, s32[1,8,64]{2,1,0:T(8,128)}, u32[]{:S(2)}) copy-start(s32[1,8,64]{2,1,0:T(8,128)} %param.13) | copy-start | bytes 6148
  15.7 26.0 %all-to-all-start = ((bf16[8,32,1024]{2,1,0:T(8,128)(2,1)}), bf16[8,32,1024]{2,1,0:T(8,128)(2,1)S(1)}, u32[]{:S(2)}, u32[]{:S(2)}) async-start(bf16[8,32,1024]{2,1,0:T(8,128)(2,1)} %select_select_fusion), calls=%async_computation | async-start | bytes 1048576 | tf_op jit(solution)/shard_map/all_to_all | solution.py:134
  24.2 223.9 %reduce-scatter.2.cloned.1.call-start = ((), (), s32[]{:S(2)}) async-start(), calls=%async_computation.4 | async-start | bytes 8921088 | tf_op jit(solution)/shard_map/reduce_scatter | solution.py:160
  110.6 3.2 copy-start.2
  110.6 3.2 copy-start.8
  113.8 1.6 copy-start.6
  132.6 3.6 %copy-start.4 = (bf16[256,1024]{1,0:T(8,128)(2,1)S(1)}, bf16[256,1024]{1,0:T(8,128)(2,1)}, u32[]{:S(2)}) copy-start(bf16[256,1024]{1,0:T(8,128)(2,1)} %reshape.305) | copy-start | bytes 1572868
  132.6 3.6 %copy-start.5 = (bf16[8,32,1024]{2,1,0:T(8,128)(2,1)S(1)}, bf16[8,32,1024]{2,1,0:T(8,128)(2,1)}, u32[]{:S(2)}) copy-start(bf16[8,32,1024]{2,1,0:T(8,128)(2,1)} %broadcast_select_fusion.1) | copy-start | bytes 1572868
  136.1 1.4 copy-start.3
  153.4 94.7 %all-to-all-start.1 = ((bf16[8,32,2048]{2,1,0:T(8,128)(2,1)}), bf16[8,32,2048]{2,1,0:T(8,128)(2,1)S(1)}, u32[]{:S(2)}, u32[]{:S(2)}) async-start(bf16[8,32,2048]{2,1,0:T(8,128)(2,1)} %broadcast_select_fusion), calls=%async_computation.1 | async-start | bytes 2097152 | tf_op jit(solution)/shard_map/all_to_all | solution.py:141
  160.4 162.8 %all-reduce.2.cloned.1.call-start = ((), (), s32[]{:S(2)}) async-start(), calls=%async_computation.5 | async-start | bytes 540672 | tf_op jit(solution)/shard_map/psum | solution.py:161
Sparse Core Ops, SparseCore 0:
  11.1 61.2 all-gather.1
  147.3 100.6 reduce-scatter.1
  250.4 72.8 all-reduce.1
where the time goes:
time: 336 us; the launch traced here: 335 us
  waiting for transfers between devices  203 us (60%)
  matrix products  44 us (13%)
  local copies, waits for them, and re-layouts  41.1 us (12%)
  other arithmetic  17.3 us (5%)
  starting transfers between devices  15.6 us (5%)
  between operations  14.1 us (4%)
    reduce_scatter x1, waiting for transfers between devices, on_device(): lax.psum_scatter(partial, 'replica', scatter_dimension=0, tiled=True)  87.6 us
    psum x1, waiting for transfers between devices, on_device(): summed = lax.psum(summed, 'batch').astype(jnp.float32)  72.4 us
    all_gather x1, waiting for transfers between devices, on_device(): lax.all_gather(jnp.concatenate([qkv_weight, out_weight, gain_block], axis...  29.1 us
    all_to_all x1, waiting for transfers between devices, on_device(): lax.all_to_all(backward_rows, 'batch', split_axis=0, concat_axis=0, tiled...  13.4 us
    all_to_all x1, starting transfers between devices, on_device(): lax.all_to_all(backward_rows, 'batch', split_axis=0, concat_axis=0, tiled...  8.47 us
    all_to_all x1, starting transfers between devices, on_device(): lax.all_to_all(jnp.take(jnp.concatenate([result, d_tokens], axis=-1), to_...  7.02 us
  transfers between devices with their start and end apart: 5, of which 4 were waited for; matrix products, arithmetic and copies ran while one was open for 6% of the time, Pallas kernels for 0%

commit v1 on v0

--- a/solution.py
+++ b/solution.py
@@ -8,6 +8,13 @@
 MEANVIS = 16
 EPS = 1e-06
 NEG = -1e30
+
+
+def build_pieces_all(load, out_dim):
+    tall = jnp.stack(jax.lax.axis_size("replica") * [load], axis=0)
+    work_now = jax.lax.all_to_all(tall, "replica", 0, 0)
+    long_array = jnp.concatenate(work_now, axis=out_dim)
+    return long_array
 
 
 def layer_core(tokens, upward, allowed, wqkv, wout, gain):
@@ -97,9 +104,7 @@
     qkv_cols = qkv_weight.shape[1]
     out_cols = out_weight.shape[1]
     gain_block = jnp.broadcast_to(norm_gain[:, None], (norm_gain.shape[0], 128))
-    gathered = lax.all_gather(
-        jnp.concatenate([qkv_weight, out_weight, gain_block], axis=1), "replica", axis=0, tiled=True
-    )
+    gathered = build_pieces_all(jnp.concatenate([qkv_weight, out_weight, gain_block], axis=1), 0)
     wqkv = gathered[:, :qkv_cols]
     wout = gathered[:, qkv_cols : qkv_cols + out_cols]
     gain = gathered[:, qkv_cols + out_cols]

time: 336 us -> 410 us (1.22)
  waiting for transfers between devices: 203 us -> 277 us
  local copies, waits for them, and re-layouts: 41.1 us -> 35.5 us
  starting transfers between devices: 15.6 us -> 19.9 us
    all_to_all x0 -> x1, waiting for transfers between devices: none -> 96.8 us  [build_pieces_all(): work_now = jax.lax.all_to_all(tall, 'replica', 0, 0)]
    all_gather x1 -> x0, waiting for transfers between devices: 29.1 us -> none  [on_device(): lax.all_gather(jnp.concatenate([qkv_weight, out_weight, gain_block], axis...]
    all_to_all x0 -> x1, starting transfers between devices: none -> 7.8 us  [build_pieces_all(): work_now = jax.lax.all_to_all(tall, 'replica', 0, 0)]
  transfers between devices with their start and end apart: 5 -> 5, of which waited for: 4 -> 4; matrix products, arithmetic and copies ran while one was open for 6% -> 3% of each run, Pallas kernels for 0% -> 0%
where the time goes in v1:
time: 410 us; the launch traced here: 409 us
  waiting for transfers between devices  277 us (68%)
  matrix products  44.8 us (11%)
  local copies, waits for them, and re-layouts  35.5 us (9%)
  starting transfers between devices  19.9 us (5%)
  other arithmetic  17.2 us (4%)
  between operations  14.4 us (4%)
    all_to_all x1, waiting for transfers between devices, build_pieces_all(): work_now = jax.lax.all_to_all(tall, 'replica', 0, 0)  96.8 us
    reduce_scatter x1, waiting for transfers between devices, on_device(): lax.psum_scatter(partial, 'replica', scatter_dimension=0, tiled=True)  90.4 us
    psum x1, waiting for transfers between devices, on_device(): summed = lax.psum(summed, 'batch').astype(jnp.float32)  72.4 us
    all_to_all x1, waiting for transfers between devices, on_device(): lax.all_to_all(backward_rows, 'batch', split_axis=0, concat_axis=0, tiled...  17.4 us
    all_to_all x1, starting transfers between devices, on_device(): lax.all_to_all(backward_rows, 'batch', split_axis=0, concat_axis=0, tiled...  8.47 us
  transfers between devices with their start and end apart: 5, of which 4 were waited for; matrix products, arithmetic and copies ran while one was open for 3% of the time, Pallas kernels for 0%

profile of v1, /device:TPU:2, one launch (start us, length us, event | category | flops | bytes accessed | tf_op | source)
XLA Modules:
  0.0 408.8 jit_solution(18375787369652851128)
XLA Ops:
  10.9 2.5 gather_fusion
  14.4 8.5 %all-to-all-start.1 = ((bf16[8,32,1024]{2,1,0:T(8,128)(2,1)}), bf16[8,32,1024]{2,1,0:T(8,128)(2,1)S(1)}, u32[]{:S(2)}, u32[]{:S(2)}) async-start(bf16[8,32,1024]{2,1,0:T(8,128)(2,1)} %select_select_fusion), calls=%async_computation.1 | async-start | bytes 1048576 | tf_op jit(solution)/shard_map/all_to_all | solution.py:139
  23.0 17.4 %all-to-all-done.1 = bf16[8,32,1024]{2,1,0:T(8,128)(2,1)S(1)} async-done(((bf16[8,32,1024]{2,1,0:T(8,128)(2,1)}), bf16[8,32,1024]{2,1,0:T(8,128)(2,1)S(1)}, u32[]{:S(2)}, u32[]{:S(2)}) %all-to-all-start.1) | async-done | bytes 524320 | tf_op jit(solution)/shard_map/all_to_all | solution.py:139
  40.4 3.9 stack.2
  44.3 7.8 %all-to-all-start = ((bf16[32,32,4224]{2,1,0:T(8,128)(2,1)}), bf16[32,32,4224]{2,1,0:T(8,128)(2,1)}, u32[]{:S(2)}, u32[]{:S(2)}) async-start(bf16[32,32,4224]{2,1,0:T(8,128)(2,1)} %stack.2), calls=%async_computation | async-start | bytes 17301504 | tf_op jit(solution)/shard_map/all_to_all | solution.py:15
  52.2 2.8 gather_fusion.3
  57.8 96.8 %all-to-all-done = bf16[32,32,4224]{2,1,0:T(8,128)(2,1)} async-done(((bf16[32,32,4224]{2,1,0:T(8,128)(2,1)}), bf16[32,32,4224]{2,1,0:T(8,128)(2,1)}, u32[]{:S(2)}, u32[]{:S(2)}) %all-to-all-start) | async-done | bytes 8650784 | tf_op jit(solution)/shard_map/all_to_all | solution.py:15
  155.7 2.3 fusion.43
  158.7 4.7 %fusion.6 = bf16[256,3072]{1,0:T(8,128)(2,1)S(1)} fusion(bf16[1024,4224]{1,0:T(8,128)(2,1)} %bitcast.5, f32[1024]{0:T(1024)S(1)} %convert_reduce_fusion.1, f32[256]{0:T(256)S(1)} %rsqrt.12, f32[256]{0:T(256)S(1)} %div.51, bf16[256,1024]{1,0:T(8,128)(2,1)S(1)} %gather_fusion.3, pred[256]{0:T(512)(128)(4,1)S(1)} %compare_and_fusion.4), kind=kOutput, calls=%fused_computation.14 | convolution fusion | flops 1612972032 | bytes 8395008 | tf_op jit(solution)/shard_map/dot_general | solution.py:34
  164.4 2.5 reshape.308
  167.0 1.6 reshape.310
  170.3 3.2 fusion.66
  173.5 4.1 fusion.111
  177.5 5.8 %fusion.34 = bf16[8,32,16,64]{3,1,2,0:T(8,128)(2,1)} fusion(f32[8,16,32,32]{2,3,1,0:T(8,128)} %fusion.66, bf16[8,32,16,64]{3,2,1,0:T(8,128)(2,1)} %reshape.310, f32[8,16,32,32]{2,3,1,0:T(8,128)} %get-tuple-element.37, f32[8,16,32]{2,1,0:T(8,128)S(1)} %get-tuple-element.36), kind=kOutput, calls=%fused_computation.35 | convolution fusion | flops 17960992 | bytes 2113536 | tf_op jit(solution)/shard_map/ghqk,gkhd->gqhd/dot_general | solution.py:62
  183.3 5.6 %fusion.31 = bf16[8,32,16,64]{3,1,2,0:T(8,128)(2,1)} fusion(f32[8,16,32,32]{2,3,1,0:T(8,128)} %fusion.66, bf16[8,32,16,64]{3,2,1,0:T(8,128)(2,1)} %reshape.309, f32[8,16,32,32]{2,3,1,0:T(8,128)} %get-tuple-element.37, f32[8,16,32]{2,1,0:T(8,128)S(1)} %get-tuple-element.36), kind=kOutput, calls=%fused_computation.34 | convolution fusion | flops 17960992 | bytes 2113536 | tf_op jit(solution)/shard_map/ghqk,gqhd->gkhd/dot_general | solution.py:65
  188.9 3.1 fusion.30
  202.2 6.3 %fusion.57 = (bf16[1024]{0:T(1024)(128)(2,1)S(1)}, f32[256]{0:T(256)S(1)}, f32[256]{0:T(256)S(1)}, f32[256,1024]{1,0:T(8,128)}) fusion(f32[256]{0:T(256)S(1)} %rsqrt.12, f32[256]{0:T(256)S(1)} %div.51, bf16[256,1024]{1,0:T(8,128)(2,1)S(1)} %gather_fusion.3, pred[256]{0:T(512)(128)(4,1)S(1)} %compare_and_fusion.4, f32[1024]{0:T(1024)S(1)} %convert_reduce_fusion.1, ...), kind=kOutput, calls=%fused_computation.53 | convolution fusion | flops 1613232640 | bytes 9447680 | tf_op jit(solution)/shard_map/dot_general | solution.py:72
  208.5 4.9 %convolution_convert_fusion = bf16[1024,3072]{1,0:T(8,128)(2,1)} fusion(bf16[256,3072]{1,0:T(8,128)(2,1)S(1)} %copy-done.3, f32[1024]{0:T(1024)S(1)} %convert_reduce_fusion.1, f32[256]{0:T(256)S(1)} %rsqrt.12, f32[256]{0:T(256)S(1)} %div.51, bf16[256,1024]{1,0:T(8,128)(2,1)S(1)} %gather_fusion.3, pred[256]{0:T(512)(128)(4,1)S(1)} %compare_and_fusion.4), kind=kOutput, calls=%fused_computation.9 | convolution fusion | flops 1615331328 | bytes 8395008 | tf_op jit(solution)/shard_map/dot_general | solution.py:96
  215.5 6.5 %pad_maximum_fusion = bf16[1024,4224]{1,0:T(8,128)(2,1)} fusion(bf16[1024,128]{1,0:T(8,128)(2,1)S(1)} %broadcast_in_dim.181, bf16[1024,1024]{1,0:T(8,128)(2,1)S(1)} %convolution_convert_fusion.1, bf16[1024,3072]{1,0:T(8,128)(2,1)} %convolution_convert_fusion), kind=kLoop, calls=%fused_computation.8 | loop fusion | flops 25952256 | bytes 17301504 | tf_op jit(solution)/shard_map/concatenate | solution.py:157
  223.8 2.3 fusion.40
  228.0 3.6 all-to-all-start.2
  231.6 90.4 %reduce-scatter.2.cloned.1.call-done = bf16[32,4224]{1,0:T(8,128)(2,1)} async-done(((bf16[1024,4224]{1,0:T(8,128)(2,1)}), bf16[32,4224]{1,0:T(8,128)(2,1)}) %reduce-scatter.2.cloned.1.call-update) | async-done | bytes 270352 | tf_op jit(solution)/shard_map/reduce_scatter | solution.py:165
  324.7 72.4 %all-reduce.2.cloned.1.call-done = bf16[32,4224]{1,0:T(8,128)(2,1)} async-done(((bf16[32,4224]{1,0:T(8,128)(2,1)}), bf16[32,4224]{1,0:T(8,128)(2,1)}) %all-reduce.2.cloned.1.call-update) | async-done | bytes 270352 | tf_op jit(solution)/shard_map/psum | solution.py:166
  398.7 1.7 slice.75
  (104 shorter events, 33.6 us)
Async XLA Ops:
  7.2 45.1 %copy-start = (bf16[1,8,64,1024]{3,2,1,0:T(8,128)(2,1)S(1)}, bf16[1,8,64,1024]{3,2,1,0:T(8,128)(2,1)}, u32[]{:S(2)}) copy-start(bf16[1,8,64,1024]{3,2,1,0:T(8,128)(2,1)} %param.12) | copy-start | bytes 3145732
  13.5 9.4 %copy-start.11 = (bf16[32]{0:T(256)(128)(2,1)S(1)}, bf16[32]{0:T(256)(128)(2,1)}, u32[]{:S(2)}) copy-start(bf16[32]{0:T(256)(128)(2,1)} %param.18) | copy-start | bytes 196
  13.5 9.5 %copy-start.8 = (bf16[32,3072]{1,0:T(8,128)(2,1)S(1)}, bf16[32,3072]{1,0:T(8,128)(2,1)}, u32[]{:S(2)}) copy-start(bf16[32,3072]{1,0:T(8,128)(2,1)} %param.16) | copy-start | bytes 589828
  13.5 9.5 %copy-start.9 = (bf16[32,1024]{1,0:T(8,128)(2,1)S(1)}, bf16[32,1024]{1,0:T(8,128)(2,1)}, u32[]{:S(2)}) copy-start(bf16[32,1024]{1,0:T(8,128)(2,1)} %param.17) | copy-start | bytes 196612
  14.4 26.0 %all-to-all-start.1 = ((bf16[8,32,1024]{2,1,0:T(8,128)(2,1)}), bf16[8,32,1024]{2,1,0:T(8,128)(2,1)S(1)}, u32[]{:S(2)}, u32[]{:S(2)}) async-start(bf16[8,32,1024]{2,1,0:T(8,128)(2,1)} %select_select_fusion), calls=%async_computation.1 | async-start | bytes 1048576 | tf_op jit(solution)/shard_map/all_to_all | solution.py:139
  44.3 7.9 %copy-start.10 = (s32[1,8,64]{2,1,0:T(8,128)S(1)}, s32[1,8,64]{2,1,0:T(8,128)}, u32[]{:S(2)}) copy-start(s32[1,8,64]{2,1,0:T(8,128)} %param.13) | copy-start | bytes 6148
  44.3 110.3 %all-to-all-start = ((bf16[32,32,4224]{2,1,0:T(8,128)(2,1)}), bf16[32,32,4224]{2,1,0:T(8,128)(2,1)}, u32[]{:S(2)}, u32[]{:S(2)}) async-start(bf16[32,32,4224]{2,1,0:T(8,128)(2,1)} %stack.2), calls=%async_computation | async-start | bytes 17301504 | tf_op jit(solution)/shard_map/all_to_all | solution.py:15
  52.1 269.9 %reduce-scatter.2.cloned.1.call-start = ((), (), s32[]{:S(2)}) async-start(), calls=%async_computation.4 | async-start | bytes 8921088 | tf_op jit(solution)/shard_map/reduce_scatter | solution.py:165
  188.9 3.2 copy-start.2
  188.9 3.2 copy-start.12
  192.1 1.6 copy-start.7
  202.2 6.3 %copy-start.3 = (bf16[256,3072]{1,0:T(8,128)(2,1)S(1)}, bf16[256,3072]{1,0:T(8,128)(2,1)}, u32[]{:S(2)}) copy-start(bf16[256,3072]{1,0:T(8,128)(2,1)} %constant_dynamic-update-slice_fusion) | copy-start | bytes 4718596
  208.5 4.9 %copy-start.6 = (bf16[8,32,16,64]{3,1,2,0:T(8,128)(2,1)S(1)}, bf16[8,32,16,64]{3,1,2,0:T(8,128)(2,1)}, u32[]{:S(2)}) copy-start(bf16[8,32,16,64]{3,1,2,0:T(8,128)(2,1)} %fusion.29) | copy-start | bytes 1572868
  213.4 1.1 copy-start.4
  222.1 1.2 copy-start.5
  228.0 94.0 %all-to-all-start.2 = ((bf16[8,32,2048]{2,1,0:T(8,128)(2,1)}), bf16[8,32,2048]{2,1,0:T(8,128)(2,1)S(1)}, u32[]{:S(2)}, u32[]{:S(2)}) async-start(bf16[8,32,2048]{2,1,0:T(8,128)(2,1)} %broadcast_select_fusion), calls=%async_computation.2 | async-start | bytes 2097152 | tf_op jit(solution)/shard_map/all_to_all | solution.py:146
  231.5 165.6 %all-reduce.2.cloned.1.call-start = ((), (), s32[]{:S(2)}) async-start(), calls=%async_computation.5 | async-start | bytes 540672 | tf_op jit(solution)/shard_map/psum | solution.py:166
  322.9 79.0 %copy-start.1 = (bf16[1,8,64,1024]{3,2,1,0:T(8,128)(2,1)S(1)}, bf16[1,8,64,1024]{3,2,1,0:T(8,128)(2,1)}, u32[]{:S(2)}) copy-start(bf16[1,8,64,1024]{3,2,1,0:T(8,128)(2,1)} %param.12) | copy-start | bytes 3145732
Sparse Core Ops, SparseCore 0:
  222.2 99.6 reduce-scatter.1
  324.3 72.7 all-reduce.1
